TPU v7x, 128 devices: a whole 4x4x4 slice. The times are simulated.
128 devices in a mesh: req: 16 (over y, z), mp: 8 (over x, core).
Axes of the slice: x: 4, y: 4, z: 4, core: 2. Of those that a mesh axis runs over, the one named last changes fastest.
Arguments:
- hidden_in: bfloat16 [16384, 2048], P('req', 'mp'), may hold values from -6 to 6
- w_qkv: bfloat16 [3, 2048, 2048], P(None, 'req', 'mp'), may hold values from -0.125 to 0.125
- w_out: bfloat16 [2048, 2048], P('mp', 'req'), may hold values from -0.125 to 0.125
- attn_gain: bfloat16 [2048], replicated, may hold values from 0.099609375 to 1.8984375
- mlp_gain: bfloat16 [2048], replicated, may hold values from 0.099609375 to 1.8984375
- w_gate: bfloat16 [2048, 8192], P('req', 'mp'), may hold values from -0.125 to 0.125
- w_up: bfloat16 [2048, 8192], P('req', 'mp'), may hold values from -0.125 to 0.125
- w_down: bfloat16 [8192, 2048], P('mp', 'req'), may hold values from -0.0625 to 0.0625
- k_cache: bfloat16 [16, 4096, 2048], P('req', None, 'mp'), may hold values from -363 to 363
- v_cache: bfloat16 [16, 4096, 2048], P('req', None, 'mp'), may hold values from -6 to 6
- cache_len: int32 [16], P('req'), may hold values from 256 to 4096, as said below
Outputs:
- hidden_out: bfloat16 [16384, 2048], P('req', 'mp')
- new_keys: bfloat16 [16384, 2048], P('req', 'mp')
- new_values: bfloat16 [16384, 2048], P('req', 'mp')
Inputs may be any that keep to these rules, and one draw needn't show every extreme that they name: Each request uses its first cache_len slots; later slots hold unused data. Some request's cache is full in every draw.
All inputs are finite; a program needn't handle non-finite values.
Results may differ from a plain program's by a relative error of at most 0.02.
Values may be sent and summed in bfloat16 or wider, within the bound.
No kernel may reach another device: no remote copies, remote signals or barrier semaphores. Data moves between devices by JAX's collectives and lax.ppermute only.
A program may use at most 128 MiB of HBM per device.

v0:
```python
import jax
import jax.numpy as jnp
from jax import lax
from jax.sharding import PartitionSpec as P

HD = 64
THETA = 130000.0
EPSILON = 1e-05
NEG_FILL = -1e30


def rms_scale(rows, gain):
    values = rows.astype(jnp.float32)
    meansq = jnp.mean(values * values, axis=-1, keepdims=True)
    return (values * lax.rsqrt(meansq + EPSILON) * gain.astype(jnp.float32)).astype(jnp.bfloat16)


def rotate(tensor, positions):
    half = tensor.shape[-1] // 2
    freq = THETA ** (-(jnp.arange(half, dtype=jnp.float32) * 2.0 / tensor.shape[-1]))
    angle = positions[:, None, None] * freq[None, None, :]
    cosine = jnp.cos(angle)
    sine = jnp.sin(angle)
    first = tensor[..., :half]
    second = tensor[..., half:]
    return jnp.concatenate(
        [first * cosine - second * sine, second * cosine + first * sine], axis=-1
    )


def absorb(carry, queries, keys, values, valid):
    top, total, accum = carry
    scores = jnp.einsum("qhd,khd->hqk", queries, keys, preferred_element_type=jnp.float32) * HD ** (
        -0.5
    )
    scores = jnp.where(valid[None], scores, NEG_FILL)
    new_top = jnp.maximum(top, jnp.max(scores, axis=-1, keepdims=True))
    factor = jnp.exp(top - new_top)
    probs = jnp.where(valid[None], jnp.exp(scores - new_top), 0.0)
    total = total * factor + jnp.sum(probs, axis=-1, keepdims=True)
    accum = accum * factor + jnp.einsum(
        "hqk,khd->hqd", probs.astype(jnp.bfloat16), values, preferred_element_type=jnp.float32
    )
    return (new_top, total, accum)


def on_device(
    hidden_in, w_qkv, w_out, attn_gain, mlp_gain, w_gate, w_up, w_down, k_cache, v_cache, cache_len
):
    new_count = hidden_in.shape[0]
    width = w_qkv.shape[2]
    heads_local = width // HD
    slots = k_cache.shape[1]
    full_rows = lax.all_gather(hidden_in, "mp", axis=1, tiled=True)
    normed = rms_scale(full_rows, attn_gain)
    columns = normed
    projected = jnp.einsum(
        "nd,kdw->knw",
        columns,
        lax.all_gather(w_qkv, "req", axis=1, tiled=True),
        preferred_element_type=jnp.float32,
    )
    length = cache_len[0]
    positions = (length + jnp.arange(new_count, dtype=jnp.int32)).astype(jnp.float32)
    queries = rotate(projected[0].reshape(new_count, heads_local, HD), positions).astype(
        jnp.bfloat16
    )
    fresh_keys = rotate(projected[1].reshape(new_count, heads_local, HD), positions).astype(
        jnp.bfloat16
    )
    fresh_values = projected[2].astype(jnp.bfloat16).reshape(new_count, heads_local, HD)
    rows = jnp.arange(new_count, dtype=jnp.int32)
    causal = rows[:, None] >= rows[None, :]
    start_carry = (
        jnp.full((heads_local, new_count, 1), NEG_FILL, jnp.float32),
        jnp.zeros((heads_local, new_count, 1), jnp.float32),
        jnp.zeros((heads_local, new_count, HD), jnp.float32),
    )
    carry = absorb(start_carry, queries, fresh_keys, fresh_values, causal)
    cache_keys = k_cache[0].reshape(slots, heads_local, HD)
    cache_values = v_cache[0].reshape(slots, heads_local, HD)
    block = min(slots, 512)
    count = (length + block - 1) // block

    def step_block(index, state):
        begin = index * block
        keys = lax.dynamic_slice_in_dim(cache_keys, begin, block, 0)
        values = lax.dynamic_slice_in_dim(cache_values, begin, block, 0)
        valid = (begin + jnp.arange(block, dtype=jnp.int32) < length)[None, :]
        return absorb(state, queries, keys, values, valid)

    top, total, accum = lax.fori_loop(0, count, step_block, carry)
    attn = (accum / total).transpose(1, 0, 2).reshape(new_count, width).astype(jnp.bfloat16)
    partial_value = jnp.dot(
        attn, lax.all_gather(w_out, "req", axis=1, tiled=True), preferred_element_type=jnp.float32
    )
    summed = lax.psum_scatter(
        partial_value.astype(jnp.bfloat16), "mp", scatter_dimension=1, tiled=True
    ).astype(jnp.float32)
    mid_local = (hidden_in.astype(jnp.float32) + summed).astype(jnp.bfloat16)
    mid_full = lax.all_gather(mid_local, "mp", axis=1, tiled=True)
    normed2 = rms_scale(mid_full, mlp_gain)
    columns = normed2
    gate = jnp.dot(
        columns,
        lax.all_gather(w_gate, "req", axis=0, tiled=True),
        preferred_element_type=jnp.float32,
    )
    upper = jnp.dot(
        columns, lax.all_gather(w_up, "req", axis=0, tiled=True), preferred_element_type=jnp.float32
    )
    units = (jax.nn.silu(gate) * upper).astype(jnp.bfloat16)
    terms = jnp.dot(
        units, lax.all_gather(w_down, "req", axis=1, tiled=True), preferred_element_type=jnp.float32
    )
    reduced = lax.psum_scatter(
        terms.astype(jnp.bfloat16), "mp", scatter_dimension=1, tiled=True
    ).astype(jnp.float32)
    hidden_out = (mid_local.astype(jnp.float32) + reduced).astype(jnp.bfloat16)
    return (
        hidden_out,
        fresh_keys.reshape(new_count, width),
        fresh_values.reshape(new_count, width),
    )


def solution(mesh):
    return jax.shard_map(
        on_device,
        mesh=mesh,
        in_specs=(
            P("req", "mp"),
            P(None, "req", "mp"),
            P("mp", "req"),
            P(),
            P(),
            P("req", "mp"),
            P("req", "mp"),
            P("mp", "req"),
            P("req", None, "mp"),
            P("req", None, "mp"),
            P("req"),
        ),
        out_specs=(P("req", "mp"), P("req", "mp"), P("req", "mp")),
        check_vma=False,
    )
```

profile of v0, /device:TPU:0, one launch (start us, length us, event | category | flops | bytes accessed | tf_op | source)
XLA Modules:
  0.0 499.0 jit_solution(9587442802145398446)
XLA Ops:
  13.1 2.9 copy.17
  16.1 4.2 copy.18
  20.8 27.4 %all-gather.8.cloned.1.call-done = bf16[1024,2048]{1,0:T(8,128)(2,1)} async-done(((bf16[1024,256]{1,0:T(8,128)(2,1)}), bf16[1024,2048]{1,0:T(8,128)(2,1)}) %all-gather.8.cloned.1.call-update) | async-done | bytes 4194320 | tf_op jit(solution)/shard_map/all_gather | solution.py:54
  48.2 3.1 fusion.23
  51.3 53.4 %all-gather.10.cloned.1.call-done = bf16[3,2048,256]{1,2,0:T(8,128)(2,1)} async-done(((bf16[3,128,256]{1,2,0:T(8,128)(2,1)}), bf16[3,2048,256]{1,2,0:T(8,128)(2,1)}) %all-gather.10.cloned.1.call-update) | async-done | bytes 3145744 | tf_op jit(solution)/shard_map/all_gather | solution.py:60
  104.7 6.6 %fusion.37 = f32[3,1024,256]{1,2,0:T(8,128)S(1)} fusion(bf16[3,2048,256]{1,2,0:T(8,128)(2,1)} %all-gather.10.cloned.1.call-done, bf16[1024,2048]{1,0:T(8,128)(2,1)} %all-gather.8.cloned.1.call-done, f32[2048]{0:T(1024)S(1)} %convert_element_type.87, f32[1024]{0:T(1024)S(1)} %add_rsqrt_fusion.1), kind=kOutput, calls=%fused_computation.49 | convolution fusion | flops 3229614080 | bytes 10498048 | tf_op jit(solution)/shard_map/nd,kdw->knw/dot_general | solution.py:57
  113.3 3.0 fusion.20
  116.4 4.2 fusion.22
  120.6 5.9 %fusion.40 = f32[4,1024,64]{1,2,0:T(8,128)} fusion(bf16[1024,4,64]{0,2,1:T(8,128)(2,1)S(1)} %bitcast.80, f32[4,1024,1024]{1,2,0:T(8,128)S(1)} %get-tuple-element.91, f32[4,1024]{1,0:T(4,128)S(1)} %get-tuple-element.87, pred[1024,1024]{0,1:T(8,128)(4,1)S(1)} %copy-done.1, f32[4,1024]{1,0:T(4,128)S(1)} %get-tuple-element.85), kind=kOutput, calls=%fused_computation.50 | convolution fusion | flops 558104576 | bytes 19431424 | tf_op jit(solution)/shard_map/hqk,khd->hqd/dot_general | solution.py:41
  126.5 8.1 %while.14 = (s32[]{:T(128)}, f32[4,1024,1]{1,0,2:T(4,128)S(1)}, f32[4,1024,1]{1,0,2:T(4,128)S(1)}, f32[4,1024,64]{1,2,0:T(8,128)}, s32[]{:T(128)}, /*index=5*/s3...) while((s32[]{:T(128)}, f32[4,1024,1]{1,0,2:T(4,128)S(1)}, ...), condition=%wide.region_6.7_spmd, body=%wide.region_3.6_spmd.sunk | while | flops 564671488 | bytes 36965104 | solution.py:92
  128.9 3.1 fusion.74
  132.0 2.5 fusion.73
  136.0 13.5 %all-gather.12.cloned.1.call-done = bf16[256,2048]{1,0:T(8,128)(2,1)} async-done(((bf16[256,128]{1,0:T(8,128)(2,1)}), bf16[256,2048]{1,0:T(8,128)(2,1)}) %all-gather.12.cloned.1.call-update) | async-done | bytes 1048592 | tf_op jit(solution)/shard_map/all_gather | solution.py:95
  149.5 4.5 convolution_convert_fusion
  154.1 79.0 %reduce-scatter.3.cloned.1.call-done = bf16[1024,256]{1,0:T(8,128)(2,1)} async-done(((bf16[1024,2048]{1,0:T(8,128)(2,1)}), bf16[1024,256]{1,0:T(8,128)(2,1)}) %reduce-scatter.3.cloned.1.call-update) | async-done | bytes 524304 | tf_op jit(solution)/shard_map/reduce_scatter | solution.py:97
  233.1 2.0 add_convert_fusion.1
  237.5 32.8 %all-gather.14.cloned.1.call-done = bf16[1024,2048]{1,0:T(8,128)(2,1)} async-done(((bf16[1024,256]{1,0:T(8,128)(2,1)}), bf16[1024,2048]{1,0:T(8,128)(2,1)}) %all-gather.14.cloned.1.call-update) | async-done | bytes 4194320 | tf_op jit(solution)/shard_map/all_gather | solution.py:101
  270.3 3.1 fusion.26
  273.4 51.6 %all-gather.16.cloned.1.call-done = bf16[2048,1024]{1,0:T(8,128)(2,1)} async-done(((bf16[128,1024]{1,0:T(8,128)(2,1)}), bf16[2048,1024]{1,0:T(8,128)(2,1)}) %all-gather.16.cloned.1.call-update) | async-done | bytes 4194320 | tf_op jit(solution)/shard_map/all_gather | solution.py:106
  325.0 10.0 %fusion.44 = f32[1024,1024]{1,0:T(8,128)} fusion(bf16[2048,1024]{1,0:T(8,128)(2,1)} %all-gather.16.cloned.1.call-done, bf16[1024,2048]{1,0:T(8,128)(2,1)} %all-gather.14.cloned.1.call-done, f32[2048]{0:T(1024)S(1)} %convert_element_type.102, f32[1024]{0:T(1024)S(1)} %add_rsqrt_fusion), kind=kOutput, calls=%fused_computation.51 | convolution fusion | flops 4303355904 | bytes 12595200 | tf_op jit(solution)/shard_map/dot_general | solution.py:104
  335.0 43.5 %all-gather.18.cloned.1.call-done = bf16[2048,1024]{1,0:T(8,128)(2,1)} async-done(((bf16[128,1024]{1,0:T(8,128)(2,1)}), bf16[2048,1024]{1,0:T(8,128)(2,1)}) %all-gather.18.cloned.1.call-update) | async-done | bytes 4194320 | tf_op jit(solution)/shard_map/all_gather | solution.py:110
  378.4 59.4 %all-gather.20.cloned.1.call-done = bf16[1024,2048]{1,0:T(8,128)(2,1)} async-done(((bf16[1024,128]{1,0:T(8,128)(2,1)}), bf16[1024,2048]{1,0:T(8,128)(2,1)}) %all-gather.20.cloned.1.call-update) | async-done | bytes 4194320 | tf_op jit(solution)/shard_map/all_gather | solution.py:114
  437.9 15.4 %convolution_convert_fusion.1 = bf16[1024,2048]{1,0:T(8,128)(2,1)} fusion(bf16[1024,2048]{1,0:T(8,128)(2,1)} %all-gather.20.cloned.1.call-done, f32[1024,1024]{1,0:T(8,128)} %fusion.44, bf16[2048,1024]{1,0:T(8,128)(2,1)} %all-gather.18.cloned.1.call-done, bf16[1024,2048]{1,0:T(8,128)(2,1)} %all-gather.14.cloned.1.call-done, ...), kind=kOutput, calls=%fused_computation.48 | convolution fusion | flops 8606711808 | bytes 20983808 | tf_op jit(solution)/shard_map/dot_general | solution.py:113
  456.6 33.9 %reduce-scatter.5.cloned.1.call-done = bf16[1024,256]{1,0:T(8,128)(2,1)} async-done(((bf16[1024,2048]{1,0:T(8,128)(2,1)}), bf16[1024,256]{1,0:T(8,128)(2,1)}) %reduce-scatter.5.cloned.1.call-update) | async-done | bytes 524304 | tf_op jit(solution)/shard_map/reduce_scatter | solution.py:116
  (59 shorter events, 19.3 us)
Async XLA Ops:
  7.2 41.0 %all-gather.8.cloned.1.call-start = ((), (), s32[]{:S(2)}) async-start(), calls=%async_computation.2 | async-start | bytes 4718592 | tf_op jit(solution)/shard_map/all_gather | solution.py:54
  7.9 96.8 %all-gather.10.cloned.1.call-start = ((), (), s32[]{:S(2)}) async-start(), calls=%async_computation.3 | async-start | bytes 3342336 | tf_op jit(solution)/shard_map/all_gather | solution.py:60
  9.7 139.8 %all-gather.12.cloned.1.call-start = ((), (), s32[]{:S(2)}) async-start(), calls=%async_computation.4 | async-start | bytes 1114112 | tf_op jit(solution)/shard_map/all_gather | solution.py:95
  10.4 222.7 %reduce-scatter.3.cloned.1.call-start = ((), (), s32[]{:S(2)}) async-start(), calls=%async_computation.5 | async-start | bytes 4718592 | tf_op jit(solution)/shard_map/reduce_scatter | solution.py:97
  111.3 1.7 copy-start.2
  111.3 2.0 copy-start.1
  126.5 2.4 copy-start.4
  132.0 2.6 copy-start.5
  134.6 98.5 %copy-start.3 = (bf16[1024,256]{1,0:T(8,128)(2,1)S(1)}, bf16[1024,256]{1,0:T(8,128)(2,1)}, u32[]{:S(2)}) copy-start(bf16[1024,256]{1,0:T(8,128)(2,1)} %param.13) | copy-start | bytes 1572868
  134.6 102.9 %copy-start.6 = (bf16[2048]{0:T(1024)(128)(2,1)S(1)}, bf16[2048]{0:T(1024)(128)(2,1)}, u32[]{:S(2)}) copy-start(bf16[2048]{0:T(1024)(128)(2,1)} %param.17) | copy-start | bytes 12292
  154.0 116.3 %all-gather.14.cloned.1.call-start = ((), (), s32[]{:S(2)}) async-start(), calls=%async_computation.6 | async-start | bytes 4718592 | tf_op jit(solution)/shard_map/all_gather | solution.py:101
  235.1 89.9 %all-gather.16.cloned.1.call-start = ((), (), s32[]{:S(2)}) async-start(), calls=%async_computation.7 | async-start | bytes 4456448 | tf_op jit(solution)/shard_map/all_gather | solution.py:106
  235.7 142.7 %all-gather.18.cloned.1.call-start = ((), (), s32[]{:S(2)}) async-start(), calls=%async_computation.8 | async-start | bytes 4456448 | tf_op jit(solution)/shard_map/all_gather | solution.py:110
  236.4 201.4 %all-gather.20.cloned.1.call-start = ((), (), s32[]{:S(2)}) async-start(), calls=%async_computation.9 | async-start | bytes 4456448 | tf_op jit(solution)/shard_map/all_gather | solution.py:114
  237.2 253.3 %reduce-scatter.5.cloned.1.call-start = ((), (), s32[]{:S(2)}) async-start(), calls=%async_computation.10 | async-start | bytes 4718592 | tf_op jit(solution)/shard_map/reduce_scatter | solution.py:116
  453.3 37.2 %copy-start = (bf16[1024,256]{1,0:T(8,128)(2,1)S(1)}, bf16[1024,256]{1,0:T(8,128)(2,1)}, u32[]{:S(2)}) copy-start(bf16[1024,256]{1,0:T(8,128)(2,1)} %add_convert_fusion.1) | copy-start | bytes 1572868
Sparse Core Ops, SparseCore 0:
  9.7 38.4 all-gather.7
  50.9 53.7 all-gather.9
  106.8 42.7 all-gather.11
  154.2 78.9 reduce-scatter.2
  235.2 35.0 all-gather.13
  272.3 52.6 all-gather.15
  327.2 51.2 all-gather.17
  380.5 57.2 all-gather.19
  453.4 37.0 reduce-scatter.4
where the time goes:
time: 500 us; the launch traced here: 499 us
  waiting for transfers between devices  398 us (80%)
  matrix products  50 us (10%)
  other arithmetic  21.9 us (4%)
  between operations  14.7 us (3%)
  local copies, waits for them, and re-layouts  13.8 us (3%)
    reduce_scatter x1, waiting for transfers between devices, on_device(): lax.psum_scatter(partial_value.astype(jnp.bfloat16), 'mp', scatter_dimens...  79 us
    all_gather x1, waiting for transfers between devices, on_device(): lax.all_gather(w_down, 'req', axis=1, tiled=True)  59.4 us
    all_gather x1, waiting for transfers between devices, on_device(): lax.all_gather(w_qkv, 'req', axis=1, tiled=True)  53.4 us
    all_gather x1, waiting for transfers between devices, on_device(): lax.all_gather(w_gate, 'req', axis=0, tiled=True)  51.6 us
    all_gather x1, waiting for transfers between devices, on_device(): lax.all_gather(w_up, 'req', axis=0, tiled=True)  43.5 us
    reduce_scatter x1, waiting for transfers between devices, on_device(): lax.psum_scatter(terms.astype(jnp.bfloat16), 'mp', scatter_dimension=1, t...  33.9 us
    all_gather x1, waiting for transfers between devices, on_device(): mid_full = lax.all_gather(mid_local, 'mp', axis=1, tiled=True)  32.8 us
    all_gather x1, waiting for transfers between devices, on_device(): full_rows = lax.all_gather(hidden_in, 'mp', axis=1, tiled=True)  27.4 us
  transfers between devices with their start and end apart: 9, of which 9 were waited for; matrix products, arithmetic and copies ran while one was open for 12% of the time, Pallas kernels for 0%

commit v1 on v0

--- a/solution.py
+++ b/solution.py
@@ -107,7 +107,11 @@
         preferred_element_type=jnp.float32,
     )
     upper = jnp.dot(
-        columns, lax.all_gather(w_up, "req", axis=0, tiled=True), preferred_element_type=jnp.float32
+        columns,
+        jnp.concatenate(
+            lax.all_to_all(jnp.stack([w_up] * lax.axis_size("req")), "req", 0, 0), axis=0
+        ),
+        preferred_element_type=jnp.float32,
     )
     units = (jax.nn.silu(gate) * upper).astype(jnp.bfloat16)
     terms = jnp.dot(

time: 500 us -> 462 us (0.924)
  waiting for transfers between devices: 398 us -> 350 us
  starting transfers between devices: 0.57 us -> 7.72 us
    all_gather x1 -> x0, waiting for transfers between devices: 43.5 us -> none  [on_device(): lax.all_gather(w_up, 'req', axis=0, tiled=True)]
    all_gather x1, waiting for transfers between devices: 51.6 us -> 66.7 us  [on_device(): lax.all_gather(w_gate, 'req', axis=0, tiled=True)]
    all_gather x1, waiting for transfers between devices: 59.4 us -> 49.5 us  [on_device(): lax.all_gather(w_down, 'req', axis=1, tiled=True)]
    all_gather x1, waiting for transfers between devices: 32.8 us -> 23.9 us  [on_device(): mid_full = lax.all_gather(mid_local, 'mp', axis=1, tiled=True)]
    all_to_all x0 -> x1, starting transfers between devices: none -> 7.18 us  [on_device(): lax.all_to_all(jnp.stack([w_up] * lax.axis_size('req')), 'req', 0, 0)]
    unnamed x15 -> x17, local copies, waits for them, and re-layouts: 12.2 us -> 12.3 us
  transfers between devices with their start and end apart: 9 -> 9, of which waited for: 9 -> 8; matrix products, arithmetic and copies ran while one was open for 12% -> 14% of each run, Pallas kernels for 0% -> 0%
where the time goes in v1:
time: 462 us; the launch traced here: 461 us
  waiting for transfers between devices  350 us (76%)
  matrix products  50 us (11%)
  other arithmetic  21.9 us (5%)
  local copies, waits for them, and re-layouts  16.3 us (4%)
  between operations  15 us (3%)
  starting transfers between devices  7.72 us (2%)
    reduce_scatter x1, waiting for transfers between devices, on_device(): lax.psum_scatter(partial_value.astype(jnp.bfloat16), 'mp', scatter_dimens...  79 us
    all_gather x1, waiting for transfers between devices, on_device(): lax.all_gather(w_gate, 'req', axis=0, tiled=True)  66.7 us
    all_gather x1, waiting for transfers between devices, on_device(): lax.all_gather(w_qkv, 'req', axis=1, tiled=True)  53.4 us
    all_gather x1, waiting for transfers between devices, on_device(): lax.all_gather(w_down, 'req', axis=1, tiled=True)  49.5 us
    reduce_scatter x1, waiting for transfers between devices, on_device(): lax.psum_scatter(terms.astype(jnp.bfloat16), 'mp', scatter_dimension=1, t...  33.9 us
    all_gather x1, waiting for transfers between devices, on_device(): full_rows = lax.all_gather(hidden_in, 'mp', axis=1, tiled=True)  27.4 us
    all_gather x1, waiting for transfers between devices, on_device(): mid_full = lax.all_gather(mid_local, 'mp', axis=1, tiled=True)  23.9 us
    dot_general x1, matrix products, on_device(): jnp.dot(units, lax.all_gather(w_down, 'req', axis=1, tiled=True), preferr...  15.3 us
  transfers between devices with their start and end apart: 9, of which 8 were waited for; matrix products, arithmetic and copies ran while one was open for 14% of the time, Pallas kernels for 0%

profile of v1, /device:TPU:0, one launch (start us, length us, event | category | flops | bytes accessed | tf_op | source)
XLA Modules:
  0.0 461.0 jit_solution(3620857353326705385)
XLA Ops:
  13.1 2.9 copy.17
  16.1 4.2 copy.18
  20.8 27.4 %all-gather.7.cloned.1.call-done = bf16[1024,2048]{1,0:T(8,128)(2,1)} async-done(((bf16[1024,256]{1,0:T(8,128)(2,1)}), bf16[1024,2048]{1,0:T(8,128)(2,1)}) %all-gather.7.cloned.1.call-update) | async-done | bytes 4194320 | tf_op jit(solution)/shard_map/all_gather | solution.py:54
  48.2 3.1 fusion.23
  51.3 53.4 %all-gather.9.cloned.1.call-done = bf16[3,2048,256]{1,2,0:T(8,128)(2,1)} async-done(((bf16[3,128,256]{1,2,0:T(8,128)(2,1)}), bf16[3,2048,256]{1,2,0:T(8,128)(2,1)}) %all-gather.9.cloned.1.call-update) | async-done | bytes 3145744 | tf_op jit(solution)/shard_map/all_gather | solution.py:60
  104.7 6.6 %fusion.37 = f32[3,1024,256]{1,2,0:T(8,128)S(1)} fusion(bf16[3,2048,256]{1,2,0:T(8,128)(2,1)} %all-gather.9.cloned.1.call-done, bf16[1024,2048]{1,0:T(8,128)(2,1)} %all-gather.7.cloned.1.call-done, f32[2048]{0:T(1024)S(1)} %convert_element_type.87, f32[1024]{0:T(1024)S(1)} %add_rsqrt_fusion.1), kind=kOutput, calls=%fused_computation.49 | convolution fusion | flops 3229614080 | bytes 10498048 | tf_op jit(solution)/shard_map/nd,kdw->knw/dot_general | solution.py:57
  113.3 3.0 fusion.20
  116.4 4.2 fusion.22
  120.6 5.9 %fusion.40 = f32[4,1024,64]{1,2,0:T(8,128)} fusion(bf16[1024,4,64]{0,2,1:T(8,128)(2,1)S(1)} %bitcast.81, f32[4,1024,1024]{1,2,0:T(8,128)S(1)} %get-tuple-element.91, f32[4,1024]{1,0:T(4,128)S(1)} %get-tuple-element.87, pred[1024,1024]{0,1:T(8,128)(4,1)S(1)} %copy-done.1, f32[4,1024]{1,0:T(4,128)S(1)} %get-tuple-element.85), kind=kOutput, calls=%fused_computation.50 | convolution fusion | flops 558104576 | bytes 19431424 | tf_op jit(solution)/shard_map/hqk,khd->hqd/dot_general | solution.py:41
  126.5 8.1 %while.14 = (s32[]{:T(128)}, f32[4,1024,1]{1,0,2:T(4,128)S(1)}, f32[4,1024,1]{1,0,2:T(4,128)S(1)}, f32[4,1024,64]{1,2,0:T(8,128)}, s32[]{:T(128)}, /*index=5*/s3...) while((s32[]{:T(128)}, f32[4,1024,1]{1,0,2:T(4,128)S(1)}, ...), condition=%wide.region_6.7_spmd, body=%wide.region_3.6_spmd.sunk | while | flops 564671488 | bytes 36965104 | solution.py:92
  128.9 3.1 fusion.74
  132.0 2.5 fusion.73
  136.0 13.5 %all-gather.11.cloned.1.call-done = bf16[256,2048]{1,0:T(8,128)(2,1)} async-done(((bf16[256,128]{1,0:T(8,128)(2,1)}), bf16[256,2048]{1,0:T(8,128)(2,1)}) %all-gather.11.cloned.1.call-update) | async-done | bytes 1048592 | tf_op jit(solution)/shard_map/all_gather | solution.py:95
  149.5 4.5 convolution_convert_fusion
  154.1 79.0 %reduce-scatter.3.cloned.1.call-done = bf16[1024,256]{1,0:T(8,128)(2,1)} async-done(((bf16[1024,2048]{1,0:T(8,128)(2,1)}), bf16[1024,256]{1,0:T(8,128)(2,1)}) %reduce-scatter.3.cloned.1.call-update) | async-done | bytes 524304 | tf_op jit(solution)/shard_map/reduce_scatter | solution.py:97
  236.5 2.5 stack.2
  239.0 7.2 %all-to-all-start = ((bf16[16,128,1024]{2,1,0:T(8,128)(2,1)}), bf16[16,128,1024]{2,1,0:T(8,128)(2,1)}, u32[]{:S(2)}, u32[]{:S(2)}) async-start(bf16[16,128,1024]{2,1,0:T(8,128)(2,1)} %stack.2), calls=%async_computation.1 | async-start | bytes 8388608 | tf_op jit(solution)/shard_map/all_to_all | solution.py:112
  246.5 23.9 %all-gather.13.cloned.1.call-done = bf16[1024,2048]{1,0:T(8,128)(2,1)} async-done(((bf16[1024,256]{1,0:T(8,128)(2,1)}), bf16[1024,2048]{1,0:T(8,128)(2,1)}) %all-gather.13.cloned.1.call-update) | async-done | bytes 4194320 | tf_op jit(solution)/shard_map/all_gather | solution.py:101
  270.4 3.1 fusion.26
  273.4 66.7 %all-gather.15.cloned.1.call-done = bf16[2048,1024]{1,0:T(8,128)(2,1)} async-done(((bf16[128,1024]{1,0:T(8,128)(2,1)}), bf16[2048,1024]{1,0:T(8,128)(2,1)}) %all-gather.15.cloned.1.call-update) | async-done | bytes 4194320 | tf_op jit(solution)/shard_map/all_gather | solution.py:106
  340.2 9.9 %fusion.44 = f32[1024,1024]{1,0:T(8,128)} fusion(bf16[2048,1024]{1,0:T(8,128)(2,1)} %all-gather.15.cloned.1.call-done, bf16[1024,2048]{1,0:T(8,128)(2,1)} %all-gather.13.cloned.1.call-done, f32[2048]{0:T(1024)S(1)} %convert_element_type.102, f32[1024]{0:T(1024)S(1)} %add_rsqrt_fusion), kind=kOutput, calls=%fused_computation.51 | convolution fusion | flops 4303355904 | bytes 12595200 | tf_op jit(solution)/shard_map/dot_general | solution.py:104
  350.1 49.5 %all-gather.17.cloned.1.call-done = bf16[1024,2048]{1,0:T(8,128)(2,1)} async-done(((bf16[1024,128]{1,0:T(8,128)(2,1)}), bf16[1024,2048]{1,0:T(8,128)(2,1)}) %all-gather.17.cloned.1.call-update) | async-done | bytes 4194320 | tf_op jit(solution)/shard_map/all_gather | solution.py:118
  399.6 15.3 %convolution_convert_fusion.1 = bf16[1024,2048]{1,0:T(8,128)(2,1)} fusion(bf16[1024,2048]{1,0:T(8,128)(2,1)} %all-gather.17.cloned.1.call-done, f32[1024,1024]{1,0:T(8,128)} %fusion.44, bf16[2048,1024]{1,0:T(8,128)(2,1)} %bitcast.18, bf16[1024,2048]{1,0:T(8,128)(2,1)} %all-gather.13.cloned.1.call-done, f32[2048]{0:T(1024)S(1)} %convert_element_type.102, ...), kind=kOutput, calls=%fused_computation.48 | convolution fusion | flops 8606711808 | bytes 20983808 | tf_op jit(solution)/shard_map/dot_general | solution.py:117
  418.3 33.9 %reduce-scatter.5.cloned.1.call-done = bf16[1024,256]{1,0:T(8,128)(2,1)} async-done(((bf16[1024,2048]{1,0:T(8,128)(2,1)}), bf16[1024,256]{1,0:T(8,128)(2,1)}) %reduce-scatter.5.cloned.1.call-update) | async-done | bytes 524304 | tf_op jit(solution)/shard_map/reduce_scatter | solution.py:120
  (61 shorter events, 20.5 us)
Async XLA Ops:
  7.2 41.0 %all-gather.7.cloned.1.call-start = ((), (), s32[]{:S(2)}) async-start(), calls=%async_computation.3 | async-start | bytes 4718592 | tf_op jit(solution)/shard_map/all_gather | solution.py:54
  7.9 96.8 %all-gather.9.cloned.1.call-start = ((), (), s32[]{:S(2)}) async-start(), calls=%async_computation.4 | async-start | bytes 3342336 | tf_op jit(solution)/shard_map/all_gather | solution.py:60
  9.7 139.8 %all-gather.11.cloned.1.call-start = ((), (), s32[]{:S(2)}) async-start(), calls=%async_computation.5 | async-start | bytes 1114112 | tf_op jit(solution)/shard_map/all_gather | solution.py:95
  10.4 222.7 %reduce-scatter.3.cloned.1.call-start = ((), (), s32[]{:S(2)}) async-start(), calls=%async_computation.6 | async-start | bytes 4718592 | tf_op jit(solution)/shard_map/reduce_scatter | solution.py:97
  111.3 1.7 copy-start.2
  111.3 2.0 copy-start.1
  126.5 2.4 copy-start.4
  132.0 2.6 copy-start.5
  134.6 98.5 %copy-start.3 = (bf16[1024,256]{1,0:T(8,128)(2,1)S(1)}, bf16[1024,256]{1,0:T(8,128)(2,1)}, u32[]{:S(2)}) copy-start(bf16[1024,256]{1,0:T(8,128)(2,1)} %param.13) | copy-start | bytes 1572868
  134.6 101.8 %copy-start.6 = (bf16[128,1024]{1,0:T(8,128)(2,1)S(1)}, bf16[128,1024]{1,0:T(8,128)(2,1)}, u32[]{:S(2)}) copy-start(bf16[128,1024]{1,0:T(8,128)(2,1)} %param.19) | copy-start | bytes 786436
  154.0 92.4 %copy-start.7 = (bf16[2048]{0:T(1024)(128)(2,1)S(1)}, bf16[2048]{0:T(1024)(128)(2,1)}, u32[]{:S(2)}) copy-start(bf16[2048]{0:T(1024)(128)(2,1)} %param.17) | copy-start | bytes 12292
  154.0 116.3 %all-gather.13.cloned.1.call-start = ((), (), s32[]{:S(2)}) async-start(), calls=%async_computation.7 | async-start | bytes 4718592 | tf_op jit(solution)/shard_map/all_gather | solution.py:101
  235.1 105.1 %all-gather.15.cloned.1.call-start = ((), (), s32[]{:S(2)}) async-start(), calls=%async_computation.8 | async-start | bytes 4456448 | tf_op jit(solution)/shard_map/all_gather | solution.py:106
  235.7 163.9 %all-gather.17.cloned.1.call-start = ((), (), s32[]{:S(2)}) async-start(), calls=%async_computation.9 | async-start | bytes 4456448 | tf_op jit(solution)/shard_map/all_gather | solution.py:118
  239.0 111.1 %all-to-all-start = ((bf16[16,128,1024]{2,1,0:T(8,128)(2,1)}), bf16[16,128,1024]{2,1,0:T(8,128)(2,1)}, u32[]{:S(2)}, u32[]{:S(2)}) async-start(bf16[16,128,1024]{2,1,0:T(8,128)(2,1)} %stack.2), calls=%async_computation.1 | async-start | bytes 8388608 | tf_op jit(solution)/shard_map/all_to_all | solution.py:112
  246.2 206.0 %reduce-scatter.5.cloned.1.call-start = ((), (), s32[]{:S(2)}) async-start(), calls=%async_computation.10 | async-start | bytes 4718592 | tf_op jit(solution)/shard_map/reduce_scatter | solution.py:120
  415.0 37.2 %copy-start = (bf16[1024,256]{1,0:T(8,128)(2,1)S(1)}, bf16[1024,256]{1,0:T(8,128)(2,1)}, u32[]{:S(2)}) copy-start(bf16[1024,256]{1,0:T(8,128)(2,1)} %add_convert_fusion.1) | copy-start | bytes 1572868
Sparse Core Ops, SparseCore 0:
  9.7 38.4 all-gather.6
  50.9 53.7 all-gather.8
  106.8 42.7 all-gather.10
  154.2 78.9 reduce-scatter.2
  235.2 35.0 all-gather.12
  272.4 67.7 all-gather.14
  342.3 57.2 all-gather.16
  415.1 37.0 reduce-scatter.4
